TPU v7x, 512 devices: a whole 4x8x8 slice. The times are simulated.
512 devices in a mesh: grp: 16 (over y, core), dom: 32 (over x, z).
Axes of the slice: x: 4, y: 8, z: 8, core: 2. Of those that a mesh axis runs over, the one named last changes fastest.
Arguments:
- owned_blips: bfloat16 [2048, 32768], P(('grp', 'dom')), may hold values from -6 to 6
- potential: float32 [32, 512, 1024], P('dom', 'grp'), may hold values from -5 to 5
- slot_owner: int32 [12288, 1], P(('grp', 'dom')), may hold values from 0 to 31; in each aligned block of 24 rows (0 to 23, 24 to 47, ...) at most 2 rows name the same one
- slot_row: int32 [12288], P(('grp', 'dom')), may hold values from 0 to 3
- slot_offset: int32 [12288], P(('grp', 'dom')), may hold values from 0 to 31
Outputs:
- blip_gradient: float32 [2048, 32768], P(('grp', 'dom'))
- hamiltonian: float32 [2048, 128], P(('grp', 'dom'))
Inputs may be any that keep to these rules, and one draw needn't show every extreme that they name: `slot_owner`: among the 24 pieces of one device at most 2 name the same owner.
All inputs are finite; a program needn't handle non-finite values.
Results may differ from a plain program's by a relative error of at most 0.012.
The roundings to bfloat16 on the way count: a program that leaves them out, or rounds other values in their place, can miss the bound.
Values may be sent and summed in bfloat16 or wider, within the bound.
No kernel may reach another device: no remote copies, remote signals or barrier semaphores. Data moves between devices by JAX's collectives and lax.ppermute only.
A program may use at most 128 MiB of HBM per device.

v0:
```python
import jax
import jax.numpy as jnp
from jax import lax
from jax.sharding import PartitionSpec as P

NB = 32


def passed_along(block, axis, distance):
    devices = range(lax.axis_size(axis))
    route = [((i - distance) % len(devices), i) for i in devices]
    return lax.ppermute(block, axis, route)


def spline_tables():
    cells_line = jnp.arange(NB, dtype=jnp.int32)
    offset = cells_line[:, None] - cells_line[None, :]
    spline = jnp.where(
        offset == 0, 2.0 / 3.0, jnp.where(jnp.abs(offset) == 1, 1.0 / 6.0, 0.0)
    ).astype(jnp.float32)
    second = jnp.where(offset == 0, -2.0, jnp.where(jnp.abs(offset) == 1, 1.0, 0.0)).astype(
        jnp.float32
    )
    plane_value = jnp.einsum("ac,bd->abcd", spline, spline).reshape(NB * NB, NB * NB)
    plane_curve = (
        jnp.einsum("ac,bd->abcd", second, spline) + jnp.einsum("ac,bd->abcd", spline, second)
    ).reshape(NB * NB, NB * NB)
    return (
        spline.astype(jnp.bfloat16),
        second.astype(jnp.bfloat16),
        plane_value.astype(jnp.bfloat16),
        plane_curve.astype(jnp.bfloat16),
    )


def on_device(owned_blips, potential, slot_owner, slot_row, slot_offset):
    spline, second, plane_value, plane_curve = spline_tables()
    domain_count = lax.axis_size("dom")
    slot_count = slot_row.shape[0]
    owned_count = owned_blips.shape[0]
    cell_count = owned_blips.shape[1]
    plane_cells = NB * NB
    capacity = max(2, -(-slot_count // domain_count))
    group_size = domain_count * owned_count
    owner_of = slot_owner[:, 0]
    target = owner_of * owned_count + slot_row
    owner_hot = (owner_of[:, None] == jnp.arange(domain_count, dtype=jnp.int32)[None, :]).astype(
        jnp.int32
    )
    position = jnp.sum(jnp.cumsum(owner_hot, axis=0) * owner_hot, axis=1) - 1
    place_slot = owner_of * capacity + position
    place_hot = place_slot[None, :] == jnp.arange(domain_count * capacity, dtype=jnp.int32)[:, None]
    asked_rows = jnp.sum(jnp.where(place_hot, slot_row[None, :], 0), axis=1) + owned_count * (
        1 - jnp.sum(place_hot.astype(jnp.int32), axis=1)
    )
    place_low = place_hot.astype(jnp.bfloat16)
    gathered_rows = lax.all_gather(owned_blips, "dom", axis=0, tiled=True)
    chosen = (
        target[:, None] == jnp.arange(gathered_rows.shape[0], dtype=jnp.int32)[None, :]
    ).astype(jnp.bfloat16)
    slot_blips = jnp.dot(chosen, gathered_rows, preferred_element_type=jnp.float32).astype(
        jnp.bfloat16
    )
    upper_cells = passed_along(potential, "grp", -1)
    extended = jnp.concatenate([potential[0], upper_cells[0]], axis=0)

    def cut_window(first_row):
        return lax.dynamic_slice_in_dim(extended, first_row, NB, 0)

    window = jax.vmap(cut_window)(slot_offset)
    layered = slot_blips.reshape(slot_count, NB, plane_cells)
    y_value = jnp.einsum("ya,sab->syb", spline, layered, preferred_element_type=jnp.float32).astype(
        jnp.bfloat16
    )
    y_curve = jnp.einsum("ya,sab->syb", second, layered, preferred_element_type=jnp.float32).astype(
        jnp.bfloat16
    )
    flat_value = y_value.reshape(-1, plane_cells)
    values_grid = jnp.dot(flat_value, plane_value, preferred_element_type=jnp.float32)
    laplace = jnp.dot(
        y_curve.reshape(-1, plane_cells), plane_value, preferred_element_type=jnp.float32
    ) + jnp.dot(flat_value, plane_curve, preferred_element_type=jnp.float32)
    applied = (-0.5 * laplace + window.reshape(-1, plane_cells) * values_grid).astype(jnp.bfloat16)
    values_low = values_grid.astype(jnp.bfloat16)
    back_plane = jnp.dot(applied, plane_value, preferred_element_type=jnp.float32).astype(
        jnp.bfloat16
    )
    gradient_piece = jnp.einsum(
        "ay,sab->syb",
        spline,
        back_plane.reshape(slot_count, NB, plane_cells),
        preferred_element_type=jnp.float32,
    ).astype(jnp.bfloat16)
    intersection = lax.dot_general(
        values_low.reshape(slot_count, cell_count),
        applied.reshape(slot_count, cell_count),
        (((1,), (1,)), ((), ())),
        preferred_element_type=jnp.float32,
    ) / float(cell_count)
    select_full = (target[:, None] == jnp.arange(group_size, dtype=jnp.int32)[None, :]).astype(
        jnp.float32
    )
    weighted = jnp.dot(intersection, select_full, precision=lax.Precision.HIGHEST)
    part_hot = (
        target[:, None] == jnp.arange(owned_count * lax.axis_size("dom"), dtype=jnp.int32)[None, :]
    ).astype(jnp.float32)
    hamilton = lax.psum_scatter(
        jnp.dot(part_hot.T, weighted, precision=lax.Precision.HIGHEST),
        "dom",
        scatter_dimension=0,
        tiled=True,
    )
    send_grad = jnp.dot(
        place_low,
        gradient_piece.reshape(slot_count, cell_count),
        preferred_element_type=jnp.bfloat16,
    ).reshape(domain_count, capacity, cell_count)
    got_grad, got_rows = (
        lax.all_to_all(send_grad, "dom", split_axis=0, concat_axis=0, tiled=True),
        lax.all_to_all(
            asked_rows.reshape(domain_count, capacity),
            "dom",
            split_axis=0,
            concat_axis=0,
            tiled=True,
        ),
    )
    owner_pick = (
        got_rows.reshape(-1)[None, :] == jnp.arange(owned_count, dtype=jnp.int32)[:, None]
    ).astype(jnp.bfloat16)
    gradient = jnp.dot(
        owner_pick, got_grad.reshape(-1, cell_count), preferred_element_type=jnp.float32
    )
    return (gradient, hamilton)


def solution(mesh):
    placed = (
        P(("grp", "dom"), None),
        P("dom", "grp", None),
        P(("grp", "dom"), None),
        P(("grp", "dom")),
        P(("grp", "dom")),
    )
    return jax.shard_map(
        on_device,
        mesh=mesh,
        in_specs=placed,
        out_specs=(P(("grp", "dom"), None), P(("grp", "dom"), None)),
        check_vma=False,
    )
```

profile of v0, /device:TPU:2, one launch (start us, length us, event | category | flops | bytes accessed | tf_op | source)
XLA Modules:
  0.0 352.7 jit_solution(15724551003374242884)
XLA Ops:
  7.9 2.9 collective-permute-start
  14.6 13.5 %all-to-all-start = ((s32[32,1,2]{2,1,0:T(1,128)}), s32[32,1,2]{2,1,0:T(1,128)S(1)}, u32[]{:S(2)}, u32[]{:S(2)}) async-start(s32[32,1,2]{2,1,0:T(1,128)} %bitcast.1), calls=%async_computation | async-start | bytes 32768 | tf_op jit(solution)/shard_map/all_to_all | solution.py:120
  28.2 7.6 %fusion.1 = (bf16[32,32,32,32]{3,2,1,0:T(8,128)(2,1)}, bf16[32,32,32,32]{3,2,1,0:T(8,128)(2,1)}) fusion(f32[32,32]{1,0:T(8,128)S(1)} %copy.33, f32[32,32]{1,0:T(8,128)S(1)} %copy.30), kind=kLoop, calls=%fused_computation.6 | loop fusion | flops 6291456 | bytes 4202496 | tf_op jit(solution)/shard_map/convert_element_type | solution.py:32
  35.9 12.4 %convert_element_type.78 = bf16[1024,1024]{1,0:T(8,128)(2,1)} reshape(bf16[32,32,32,32]{3,2,1,0:T(8,128)(2,1)} %get-tuple-element.21) | data formatting | bytes 4194304 | tf_op jit(solution)/shard_map/convert_element_type | solution.py:31
  48.3 11.4 %convert_element_type.84 = bf16[1024,1024]{1,0:T(8,128)(2,1)S(1)} reshape(bf16[32,32,32,32]{3,2,1,0:T(8,128)(2,1)} %get-tuple-element.20) | data formatting | bytes 4194304 | tf_op jit(solution)/shard_map/convert_element_type | solution.py:32
  59.8 48.0 %while.1 = (s32[]{:T(128)}, f32[64,1024]{1,0:T(8,128)S(1)}, s32[24,2]{0,1:T(2,128)S(1)}, f32[24,32,1024]{2,1,0:T(8,128)}, s32[]{:T(128)}) while((s32[]{:T(128)}, f32[64,1024]{1,0:T(8,128)S(1)}, s32[24,2]{0,1:T(2,128)S(1)}, f32[24,32,1024]{2,1,0:T(8,128)}, s32[]{:T(128)}) %tuple.24), condition=%wide.while_cond, body=%wide.while_body.sunk | while | flops 2 | bytes 263257 | solution.py:68
  60.4 1.3 bitcast_dynamic-update-slice_fusion.2
  64.4 1.3 bitcast_dynamic-update-slice_fusion.2
  66.4 1.4 bitcast_dynamic-update-slice_fusion.2
  70.4 1.3 bitcast_dynamic-update-slice_fusion.2
  72.4 1.3 bitcast_dynamic-update-slice_fusion.2
  78.4 1.3 bitcast_dynamic-update-slice_fusion.2
  82.4 1.4 bitcast_dynamic-update-slice_fusion.2
  84.4 1.3 bitcast_dynamic-update-slice_fusion.2
  90.4 1.4 bitcast_dynamic-update-slice_fusion.2
  96.4 1.3 bitcast_dynamic-update-slice_fusion.2
  100.4 1.3 bitcast_dynamic-update-slice_fusion.2
  104.4 1.3 bitcast_dynamic-update-slice_fusion.2
  107.7 10.9 %all-gather.3.cloned.1.call-done = bf16[32,4,32768]{2,1,0:T(4,128)(2,1)} async-done(((bf16[1,4,32768]{2,1,0:T(4,128)(2,1)}), bf16[32,4,32768]{2,1,0:T(4,128)(2,1)}) %all-gather.3.cloned.1.call-update) | async-done | bytes 8388624 | tf_op jit(solution)/shard_map/all_gather | solution.py:57
  118.6 12.7 %reshape.131 = bf16[128,32768]{1,0:T(8,128)(2,1)} reshape(bf16[32,4,32768]{2,1,0:T(4,128)(2,1)} %all-gather.3.cloned.1.call-done) | data formatting | bytes 16777216
  131.3 4.6 %convolution_convert_fusion = bf16[24,32768]{1,0:T(8,128)(2,1)S(1)} fusion(bf16[128,32768]{1,0:T(8,128)(2,1)} %reshape.131, s32[24]{0:T(128)S(1)} %get-tuple-element.23), kind=kOutput, calls=%fused_computation.2 | convolution fusion | flops 202116096 | bytes 9961568 | tf_op jit(solution)/shard_map/dot_general | solution.py:61
  139.0 3.0 fusion.41
  142.1 1.8 fusion.42
  143.9 1.9 fusion.3
  145.9 1.8 convolution_convert_fusion.4
  149.2 1.4 fusion.5
  150.6 6.3 %copy.35 = bf16[32,2,32768]{2,1,0:T(2,128)(2,1)} copy(bf16[32,2,32768]{2,0,1:T(8,128)(2,1)S(1)} %fusion.5) | data formatting | bytes 8388608 | tf_op jit(solution)/shard_map/dot_general | solution.py:113
  156.9 7.2 %all-to-all-start.1 = ((bf16[32,2,32768]{2,1,0:T(2,128)(2,1)}), bf16[32,2,32768]{2,1,0:T(2,128)(2,1)}, u32[]{:S(2)}, u32[]{:S(2)}) async-start(bf16[32,2,32768]{2,1,0:T(2,128)(2,1)} %copy.35), calls=%async_computation.1 | async-start | bytes 8388608 | tf_op jit(solution)/shard_map/all_to_all | solution.py:119
  164.9 2.6 reshape.109
  172.6 161.1 %all-reduce.4.cloned.1.call-done = f32[128,128]{1,0:T(8,128)} async-done(((f32[128,128]{1,0:T(8,128)}), f32[128,128]{1,0:T(8,128)}) %all-reduce.4.cloned.1.call-update) | async-done | bytes 65552
  334.9 7.3 %reshape.108 = bf16[64,32768]{1,0:T(8,128)(2,1)} reshape(bf16[32,2,32768]{2,1,0:T(2,128)(2,1)} %all-to-all-done.1) | data formatting | bytes 8388608 | tf_op jit(solution)/shard_map/reshape | solution.py:132
  342.2 3.6 %fusion.23 = f32[4,32768]{1,0:T(4,128)} fusion(bf16[64,32768]{1,0:T(8,128)(2,1)} %reshape.108, s32[64]{0:T(128)S(1)} %eq.115), kind=kOutput, calls=%fused_computation.45 | convolution fusion | flops 16777472 | bytes 4718848 | tf_op jit(solution)/shard_map/dot_general | solution.py:131
  (109 shorter events, 47.6 us)
Async XLA Ops:
  7.2 111.5 %all-gather.3.cloned.1.call-start = ((), (), s32[]{:S(2)}) async-start(), calls=%async_computation.2 | async-start | bytes 8650752 | tf_op jit(solution)/shard_map/all_gather | solution.py:57
  7.9 51.8 %collective-permute-start = (f32[1,32,1024]{2,1,0:T(8,128)}, f32[1,32,1024]{2,1,0:T(8,128)S(1)}, u32[]{:S(2)}, u32[]{:S(2)}) collective-permute-start(f32[1,32,1024]{2,1,0:T(8,128)} %param.6), channel_id=1, source_target_pairs={{32,0},{64,32},{96,64},{128,96},{160,128},{192,160},{224,192},{256... | collective-permute-start | bytes 393224 | tf_op jit(solution)/shard_map/ppermute | solution.py:12
  14.6 142.3 %all-to-all-start = ((s32[32,1,2]{2,1,0:T(1,128)}), s32[32,1,2]{2,1,0:T(1,128)S(1)}, u32[]{:S(2)}, u32[]{:S(2)}) async-start(s32[32,1,2]{2,1,0:T(1,128)} %bitcast.1), calls=%async_computation | async-start | bytes 32768 | tf_op jit(solution)/shard_map/all_to_all | solution.py:120
  28.2 7.6 %copy-start.5 = (s32[24]{0:T(128)S(1)}, s32[24]{0:T(128)}, u32[]{:S(2)}) copy-start(s32[24]{0:T(128)} %param.9) | copy-start | bytes 292
  48.3 11.4 %copy-start.4 = (f32[1,32,1024]{2,1,0:T(8,128)S(1)}, f32[1,32,1024]{2,1,0:T(8,128)}, u32[]{:S(2)}) copy-start(f32[1,32,1024]{2,1,0:T(8,128)} %param.6) | copy-start | bytes 393220
  137.4 1.6 copy-start.3
  142.1 1.9 copy-start.2
  145.9 1.8 copy-start
  156.9 7.3 %copy-start.1 = (bf16[768,1024]{1,0:T(8,128)(2,1)S(1)}, bf16[768,1024]{1,0:T(8,128)(2,1)}, u32[]{:S(2)}) copy-start(bf16[768,1024]{1,0:T(8,128)(2,1)} %copy-done) | copy-start | bytes 4718596
  156.9 178.1 %all-to-all-start.1 = ((bf16[32,2,32768]{2,1,0:T(2,128)(2,1)}), bf16[32,2,32768]{2,1,0:T(2,128)(2,1)}, u32[]{:S(2)}, u32[]{:S(2)}) async-start(bf16[32,2,32768]{2,1,0:T(2,128)(2,1)} %copy.35), calls=%async_computation.1 | async-start | bytes 8388608 | tf_op jit(solution)/shard_map/all_to_all | solution.py:119
  164.1 169.6 %all-reduce.4.cloned.1.call-start = ((), (), s32[]{:S(2)}) async-start(), calls=%async_computation.3 | async-start | bytes 131072
Sparse Core Ops, SparseCore 0:
  11.1 107.4 all-gather.2
  169.4 164.1 all-reduce.3
where the time goes:
time: 354 us; the launch traced here: 353 us
  waiting for transfers between devices  173 us (49%)
  local copies, waits for them, and re-layouts  108 us (31%)
  starting transfers between devices  23.7 us (7%)
  matrix products  21.8 us (6%)
  between operations  14.9 us (4%)
  other arithmetic  11.4 us (3%)
    unnamed x3, waiting for transfers between devices  162 us
    gather x72, local copies, waits for them, and re-layouts  47.9 us
    unnamed x16, local copies, waits for them, and re-layouts  17.1 us
    all_to_all x1, starting transfers between devices, on_device(): lax.all_to_all(asked_rows.reshape(domain_count, capacity), 'dom', split_a...  13.5 us
    convert_element_type x1, local copies, waits for them, and re-layouts, spline_tables(): plane_value.astype(jnp.bfloat16)  12.4 us
    convert_element_type x1, local copies, waits for them, and re-layouts, spline_tables(): plane_curve.astype(jnp.bfloat16)  11.4 us
    all_gather x1, waiting for transfers between devices, on_device(): gathered_rows = lax.all_gather(owned_blips, 'dom', axis=0, tiled=True)  10.9 us
    convert_element_type x1, other arithmetic, spline_tables(): plane_curve.astype(jnp.bfloat16)  7.61 us
  transfers between devices with their start and end apart: 5, of which 2 were waited for; matrix products, arithmetic and copies ran while one was open for 37% of the time, Pallas kernels for 0%

commit v1 on v0

--- a/solution.py
+++ b/solution.py
@@ -54,7 +54,8 @@
         1 - jnp.sum(place_hot.astype(jnp.int32), axis=1)
     )
     place_low = place_hot.astype(jnp.bfloat16)
-    gathered_rows = lax.all_gather(owned_blips, "dom", axis=0, tiled=True)
+    copies = jnp.concatenate([owned_blips] * lax.axis_size("dom"), axis=0)
+    gathered_rows = lax.all_to_all(copies, "dom", 0, 0, tiled=True)
     chosen = (
         target[:, None] == jnp.arange(gathered_rows.shape[0], dtype=jnp.int32)[None, :]
     ).astype(jnp.bfloat16)

time: 354 us -> 527 us (1.49)
  waiting for transfers between devices: 173 us -> 261 us
  local copies, waits for them, and re-layouts: 108 us -> 175 us
  starting transfers between devices: 23.7 us -> 40.5 us
    all_to_all x0 -> x1, waiting for transfers between devices: none -> 101 us  [on_device(): gathered_rows = lax.all_to_all(copies, 'dom', 0, 0, tiled=True)]
    concatenate x0 -> x1, local copies, waits for them, and re-layouts: none -> 53.4 us  [on_device(): copies = jnp.concatenate([owned_blips] * lax.axis_size('dom'), axis=0)]
    all_to_all x0 -> x2, local copies, waits for them, and re-layouts: none -> 25.7 us  [on_device(): gathered_rows = lax.all_to_all(copies, 'dom', 0, 0, tiled=True)]
    all_to_all x0 -> x1, starting transfers between devices: none -> 13.7 us  [on_device(): gathered_rows = lax.all_to_all(copies, 'dom', 0, 0, tiled=True)]
    unnamed x16 -> x19, local copies, waits for them, and re-layouts: 17.1 us -> 4.41 us
    all_gather x1 -> x0, waiting for transfers between devices: 10.9 us -> none  [on_device(): gathered_rows = lax.all_gather(owned_blips, 'dom', axis=0, tiled=True)]
    unnamed x3 -> x2, waiting for transfers between devices: 162 us -> 160 us
  transfers between devices with their start and end apart: 5 -> 5, of which waited for: 2 -> 2; matrix products, arithmetic and copies ran while one was open for 37% -> 22% of each run, Pallas kernels for 0% -> 0%
where the time goes in v1:
time: 527 us; the launch traced here: 522 us
  waiting for transfers between devices  261 us (50%)
  local copies, waits for them, and re-layouts  175 us (33%)
  starting transfers between devices  40.5 us (8%)
  matrix products  21.8 us (4%)
  between operations  14.9 us (3%)
  other arithmetic  8.72 us (2%)
    unnamed x2, waiting for transfers between devices  160 us
    all_to_all x1, waiting for transfers between devices, on_device(): gathered_rows = lax.all_to_all(copies, 'dom', 0, 0, tiled=True)  101 us
    concatenate x1, local copies, waits for them, and re-layouts, on_device(): copies = jnp.concatenate([owned_blips] * lax.axis_size('dom'), axis=0)  53.4 us
    gather x72, local copies, waits for them, and re-layouts  48.4 us
    all_to_all x2, local copies, waits for them, and re-layouts, on_device(): gathered_rows = lax.all_to_all(copies, 'dom', 0, 0, tiled=True)  25.7 us
    all_to_all x1, starting transfers between devices, on_device(): lax.all_to_all(asked_rows.reshape(domain_count, capacity), 'dom', split_a...  14.4 us
    all_to_all x1, starting transfers between devices, on_device(): gathered_rows = lax.all_to_all(copies, 'dom', 0, 0, tiled=True)  13.7 us
    convert_element_type x1, local copies, waits for them, and re-layouts, spline_tables(): plane_value.astype(jnp.bfloat16)  12.4 us
  transfers between devices with their start and end apart: 5, of which 2 were waited for; matrix products, arithmetic and copies ran while one was open for 22% of the time, Pallas kernels for 0%

profile of v1, /device:TPU:2, one launch (start us, length us, event | category | flops | bytes accessed | tf_op | source)
XLA Modules:
  0.0 522.4 jit_solution(16077072969938248982)
XLA Ops:
  7.2 53.4 %concatenate.9 = bf16[128,32768]{1,0:T(8,128)(2,1)} concatenate(bf16[4,32768]{1,0:T(4,128)(2,1)} %param.5, bf16[4,32768]{1,0:T(4,128)(2,1)} %param.5, bf16[4,32768]{1,0:T(4,128)(2,1)} %param.5, bf16[4,32768]{1,0:T(4,128)(2,1)} %param.5, bf16[4,32768]{1,0:T(4,128)(2,1)} %param.5, bf16[4,32768]{1,0:T(4,128)(2,1)} %param.5, bf16[4,32768]{1,0:T(4,128)(2,1)} %param.5, ...), dimensions={0} | concatenate | bytes 16777216 | tf_op jit(solution)/shard_map/concatenate | solution.py:57
  60.6 13.0 %all_to_all.16 = bf16[32,4,32768]{2,1,0:T(4,128)(2,1)} reshape(bf16[128,32768]{1,0:T(8,128)(2,1)} %concatenate.9) | data formatting | bytes 16777216 | tf_op jit(solution)/shard_map/all_to_all | solution.py:58
  73.6 13.7 %all-to-all-start.1 = ((bf16[32,4,32768]{2,1,0:T(4,128)(2,1)}), bf16[32,4,32768]{2,1,0:T(4,128)(2,1)}, u32[]{:S(2)}, u32[]{:S(2)}) async-start(bf16[32,4,32768]{2,1,0:T(4,128)(2,1)} %all_to_all.16), calls=%async_computation.1 | async-start | bytes 16777216 | tf_op jit(solution)/shard_map/all_to_all | solution.py:58
  87.3 2.4 collective-permute-start
  90.3 7.6 %fusion.1 = (bf16[32,32,32,32]{3,2,1,0:T(8,128)(2,1)}, bf16[32,32,32,32]{3,2,1,0:T(8,128)(2,1)}) fusion(f32[32,32]{1,0:T(8,128)S(1)} %copy.33, f32[32,32]{1,0:T(8,128)S(1)} %copy.30), kind=kLoop, calls=%fused_computation.6 | loop fusion | flops 6291456 | bytes 4202496 | tf_op jit(solution)/shard_map/convert_element_type | solution.py:32
  97.9 12.4 %convert_element_type.78 = bf16[1024,1024]{1,0:T(8,128)(2,1)} reshape(bf16[32,32,32,32]{3,2,1,0:T(8,128)(2,1)} %get-tuple-element.21) | data formatting | bytes 4194304 | tf_op jit(solution)/shard_map/convert_element_type | solution.py:31
  110.3 11.3 %convert_element_type.84 = bf16[1024,1024]{1,0:T(8,128)(2,1)S(1)} reshape(bf16[32,32,32,32]{3,2,1,0:T(8,128)(2,1)} %get-tuple-element.20) | data formatting | bytes 4194304 | tf_op jit(solution)/shard_map/convert_element_type | solution.py:32
  122.4 48.5 %while.1 = (s32[]{:T(128)}, f32[64,1024]{1,0:T(8,128)S(1)}, s32[24,2]{0,1:T(2,128)S(1)}, f32[24,32,1024]{2,1,0:T(8,128)}, s32[]{:T(128)}) while((s32[]{:T(128)}, f32[64,1024]{1,0:T(8,128)S(1)}, s32[24,2]{0,1:T(2,128)S(1)}, f32[24,32,1024]{2,1,0:T(8,128)}, s32[]{:T(128)}) %tuple.24), condition=%wide.while_cond, body=%wide.while_body.sunk | while | flops 2 | bytes 263257 | solution.py:69
  129.1 1.4 bitcast_dynamic-update-slice_fusion.2
  133.1 1.4 bitcast_dynamic-update-slice_fusion.2
  135.1 1.4 bitcast_dynamic-update-slice_fusion.2
  137.2 1.4 bitcast_dynamic-update-slice_fusion.2
  139.2 1.4 bitcast_dynamic-update-slice_fusion.2
  151.3 1.4 bitcast_dynamic-update-slice_fusion.2
  155.3 1.4 bitcast_dynamic-update-slice_fusion.2
  159.4 1.4 bitcast_dynamic-update-slice_fusion.2
  161.4 1.4 bitcast_dynamic-update-slice_fusion.2
  163.4 1.4 bitcast_dynamic-update-slice_fusion.2
  170.8 101.2 %all-to-all-done.1 = bf16[32,4,32768]{2,1,0:T(4,128)(2,1)} async-done(((bf16[32,4,32768]{2,1,0:T(4,128)(2,1)}), bf16[32,4,32768]{2,1,0:T(4,128)(2,1)}, u32[]{:S(2)}, u32[]{:S(2)}) %all-to-all-start.1) | async-done | bytes 8388640 | tf_op jit(solution)/shard_map/all_to_all | solution.py:58
  272.0 14.4 %all-to-all-start = ((s32[32,1,2]{2,1,0:T(1,128)}), s32[32,1,2]{2,1,0:T(1,128)S(1)}, u32[]{:S(2)}, u32[]{:S(2)}) async-start(s32[32,1,2]{2,1,0:T(1,128)} %bitcast.1), calls=%async_computation | async-start | bytes 32768 | tf_op jit(solution)/shard_map/all_to_all | solution.py:121
  286.5 12.7 %all_to_all.18 = bf16[128,32768]{1,0:T(8,128)(2,1)} reshape(bf16[32,4,32768]{2,1,0:T(4,128)(2,1)} %all-to-all-done.1) | data formatting | bytes 16777216 | tf_op jit(solution)/shard_map/all_to_all | solution.py:58
  299.1 4.6 convolution_convert_fusion
  306.9 3.0 fusion.41
  309.9 1.8 fusion.42
  311.8 1.9 fusion.3
  313.7 1.8 convolution_convert_fusion.4
  318.5 6.3 %copy.35 = bf16[32,2,32768]{2,1,0:T(2,128)(2,1)} copy(bf16[32,2,32768]{2,0,1:T(8,128)(2,1)S(1)} %fusion.5) | data formatting | bytes 8388608 | tf_op jit(solution)/shard_map/dot_general | solution.py:114
  324.8 10.0 %all-to-all-start.2 = ((bf16[32,2,32768]{2,1,0:T(2,128)(2,1)}), bf16[32,2,32768]{2,1,0:T(2,128)(2,1)}, u32[]{:S(2)}, u32[]{:S(2)}) async-start(bf16[32,2,32768]{2,1,0:T(2,128)(2,1)} %copy.35), calls=%async_computation.2 | async-start | bytes 8388608 | tf_op jit(solution)/shard_map/all_to_all | solution.py:120
  335.6 2.6 reshape.111
  343.2 160.2 %all-reduce.4.cloned.1.call-done = f32[128,128]{1,0:T(8,128)} async-done(((f32[128,128]{1,0:T(8,128)}), f32[128,128]{1,0:T(8,128)}) %all-reduce.4.cloned.1.call-update) | async-done | bytes 65552
  504.7 7.3 %reshape.110 = bf16[64,32768]{1,0:T(8,128)(2,1)} reshape(bf16[32,2,32768]{2,1,0:T(2,128)(2,1)} %all-to-all-done.2) | data formatting | bytes 8388608 | tf_op jit(solution)/shard_map/reshape | solution.py:133
  512.0 3.6 fusion.23
  (114 shorter events, 48.7 us)
Async XLA Ops:
  73.6 13.7 %copy-start.4 = (f32[1,32,1024]{2,1,0:T(8,128)S(1)}, f32[1,32,1024]{2,1,0:T(8,128)}, u32[]{:S(2)}) copy-start(f32[1,32,1024]{2,1,0:T(8,128)} %param.6) | copy-start | bytes 393220
  73.6 16.2 %copy-start.5 = (s32[24,1]{0,1:T(1,128)S(1)}, s32[24,1]{0,1:T(1,128)}, u32[]{:S(2)}) copy-start(s32[24,1]{0,1:T(1,128)} %param.7) | copy-start | bytes 292
  73.6 16.5 %copy-start.6 = (s32[24]{0:T(128)S(1)}, s32[24]{0:T(128)}, u32[]{:S(2)}) copy-start(s32[24]{0:T(128)} %param.8) | copy-start | bytes 292
  73.6 198.4 %all-to-all-start.1 = ((bf16[32,4,32768]{2,1,0:T(4,128)(2,1)}), bf16[32,4,32768]{2,1,0:T(4,128)(2,1)}, u32[]{:S(2)}, u32[]{:S(2)}) async-start(bf16[32,4,32768]{2,1,0:T(4,128)(2,1)} %all_to_all.16), calls=%async_computation.1 | async-start | bytes 16777216 | tf_op jit(solution)/shard_map/all_to_all | solution.py:58
  87.3 35.0 %collective-permute-start = (f32[1,32,1024]{2,1,0:T(8,128)S(1)}, f32[1,32,1024]{2,1,0:T(8,128)S(1)}, u32[]{:S(2)}, u32[]{:S(2)}) collective-permute-start(f32[1,32,1024]{2,1,0:T(8,128)S(1)} %copy-done.4), channel_id=1, source_target_pairs={{32,0},{64,32},{96,64},{128,96},{160,128},{192,160},{224,192},{256... | collective-permute-start | bytes 393224 | tf_op jit(solution)/shard_map/ppermute | solution.py:12
  90.3 7.6 %copy-start.7 = (s32[24]{0:T(128)S(1)}, s32[24]{0:T(128)}, u32[]{:S(2)}) copy-start(s32[24]{0:T(128)} %param.9) | copy-start | bytes 292
  272.0 52.7 %all-to-all-start = ((s32[32,1,2]{2,1,0:T(1,128)}), s32[32,1,2]{2,1,0:T(1,128)S(1)}, u32[]{:S(2)}, u32[]{:S(2)}) async-start(s32[32,1,2]{2,1,0:T(1,128)} %bitcast.1), calls=%async_computation | async-start | bytes 32768 | tf_op jit(solution)/shard_map/all_to_all | solution.py:121
  305.3 1.6 copy-start.3
  309.9 1.9 copy-start.2
  313.7 1.8 copy-start
  324.8 10.0 %copy-start.1 = (bf16[768,1024]{1,0:T(8,128)(2,1)S(1)}, bf16[768,1024]{1,0:T(8,128)(2,1)}, u32[]{:S(2)}) copy-start(bf16[768,1024]{1,0:T(8,128)(2,1)} %copy-done) | copy-start | bytes 4718596
  324.8 179.9 %all-to-all-start.2 = ((bf16[32,2,32768]{2,1,0:T(2,128)(2,1)}), bf16[32,2,32768]{2,1,0:T(2,128)(2,1)}, u32[]{:S(2)}, u32[]{:S(2)}) async-start(bf16[32,2,32768]{2,1,0:T(2,128)(2,1)} %copy.35), calls=%async_computation.2 | async-start | bytes 8388608 | tf_op jit(solution)/shard_map/all_to_all | solution.py:120
  334.7 168.7 %all-reduce.4.cloned.1.call-start = ((), (), s32[]{:S(2)}) async-start(), calls=%async_computation.3 | async-start | bytes 131072
Sparse Core Ops, SparseCore 0:
  340.1 163.2 all-reduce.3
